TPU v7x, 32 devices: a whole 2x2x4 slice. The times are simulated.
32 devices in a mesh: ctx: 8 (over y, x, core), tp: 4 (over z).
Axes of the slice: x: 2, y: 2, z: 4, core: 2. Of those that a mesh axis runs over, the one named last changes fastest.
Arguments:
- tokens: bfloat16 [4096, 4096], P(('ctx', 'tp')), may hold values from -6 to 6
- spike_query: int32 [4096, 32], P('ctx', 'tp'), may hold values 0 or 1
- spike_key: int32 [4096, 32], P('ctx', 'tp'), may hold values 0 or 1
- qkv_weight: bfloat16 [4096, 3, 4096], P(None, None, 'tp'), may hold values from -0.09375 to 0.09375
- qkv_blocks: int32 [3, 32, 32], P(None, None, 'tp'), may hold values 0 or 1
- out_weight: bfloat16 [4096, 4096], P('tp'), may hold values from -0.09375 to 0.09375
- out_blocks: int32 [32, 32], P('tp'), may hold values 0 or 1
- cotangent: bfloat16 [4096, 4096], P(('ctx', 'tp')), may hold values from -6 to 6
Outputs:
- layer_out: bfloat16 [4096, 4096], P(('ctx', 'tp'))
- token_grad: bfloat16 [4096, 4096], P(('ctx', 'tp'))
- qkv_grad: float32 [4096, 3, 4096], P('ctx', None, 'tp')
- out_grad: float32 [4096, 4096], P('tp', 'ctx')
All inputs are finite; a program needn't handle non-finite values. No bound on the sum of `spike_query` or of `spike_key` or of `qkv_blocks` or of `out_blocks` on one device may be relied on, other than what follows from the above.
Results may differ from a plain program's by a relative error of at most 0.014.
Values may be sent and summed in bfloat16 or wider, within the bound.
No kernel may reach another device: no remote copies, remote signals or barrier semaphores. Data moves between devices by JAX's collectives and lax.ppermute only.
A program may use at most 320 MiB of HBM per device.

v0:
```python
import math
import jax
import jax.numpy as jnp
from jax import lax
from jax.sharding import PartitionSpec as P

BLOCK = 128
EPSILON = 1e-05


def carried_in(value, axis, join, neutral):
    place = lax.axis_index(axis)
    gathered = lax.all_gather(value.astype(jnp.bfloat16), axis)
    state = jnp.zeros_like(value) + jnp.asarray(neutral, value.dtype)

    def carried_one(lap, state):
        return join(state, lax.dynamic_index_in_dim(gathered, lap, 0, False).astype(value.dtype))

    return lax.fori_loop(0, place, carried_one, state)


def entering(value, axis, join, neutral):
    count = lax.axis_size(axis)
    place = lax.axis_index(axis)
    ahead = count - 1 - place
    gathered = lax.all_gather(
        value.astype(jnp.bfloat16 if value.dtype == jnp.float32 else value.dtype), axis
    )
    state = jnp.zeros_like(value) + jnp.asarray(neutral, value.dtype)

    def entering_one(lap, state):
        source = count - 1 - lap
        return join(state, lax.dynamic_index_in_dim(gathered, source, 0, False).astype(value.dtype))

    return lax.fori_loop(0, ahead, entering_one, state)


def expand_blocks(blocks):
    row_blocks, col_blocks = blocks.shape
    spread = jnp.broadcast_to(
        blocks.astype(jnp.bfloat16)[:, None, :, None], (row_blocks, BLOCK, col_blocks, BLOCK)
    )
    return spread.reshape(row_blocks * BLOCK, col_blocks * BLOCK)


def qkv_keep_table(qkv_blocks):
    tables = [expand_blocks(qkv_blocks[projection]) for projection in range(3)]
    return jnp.stack(tables, axis=1)


def add_states(earlier, following):
    return earlier + following


def on_device(
    tokens, spike_query, spike_key, qkv_weight, qkv_blocks, out_weight, out_blocks, cotangent
):
    model_width = tokens.shape[1]
    block_rows = spike_query.shape[0]
    local_heads = spike_query.shape[1]
    features = qkv_weight.shape[2]
    head_width = features // local_heads
    highest = lax.Precision.HIGHEST
    qkv_keep = qkv_keep_table(qkv_blocks).reshape(model_width, 3 * features)
    qkv_used = qkv_weight.reshape(model_width, 3 * features) * qkv_keep
    out_used = out_weight * expand_blocks(out_blocks)
    gathered = lax.all_gather(tokens, "tp", axis=0, tiled=True)
    projected = jnp.dot(gathered, qkv_used, preferred_element_type=jnp.float32).astype(jnp.bfloat16)
    projected = projected.reshape(block_rows, 3, local_heads, head_width)
    query_spikes = spike_query.astype(jnp.bfloat16)[:, :, None]
    key_spikes = spike_key.astype(jnp.bfloat16)[:, :, None]
    query_spiked = projected[:, 0] * query_spikes
    key_spiked = projected[:, 1] * key_spikes
    values = projected[:, 2]
    query_wide = query_spiked.astype(jnp.float32)
    key_wide = key_spiked.astype(jnp.float32)
    local_state = jnp.einsum("shd,she->hde", key_spiked, values, preferred_element_type=jnp.float32)
    zeros_state = jnp.zeros_like(local_state)
    prior_state = carried_in(local_state, "ctx", add_states, zeros_state)
    positions = lax.iota(jnp.int32, block_rows)
    causal_keep = positions[:, None] >= positions[None, :]
    scores = jnp.einsum(
        "thd,shd->hts", query_spiked, key_spiked, preferred_element_type=jnp.float32
    )
    scores = jnp.where(causal_keep, scores, 0.0).astype(jnp.bfloat16)
    mixed_rows = jnp.einsum("hts,she->the", scores, values, preferred_element_type=jnp.float32)
    mixed_rows = mixed_rows + jnp.einsum("thd,hde->the", query_wide, prior_state, precision=highest)
    inv_rms = lax.rsqrt(jnp.mean(mixed_rows * mixed_rows, axis=-1, keepdims=True) + EPSILON)
    normed = mixed_rows * inv_rms
    attended = normed.astype(jnp.bfloat16).reshape(block_rows, features)
    row_piece = attended
    head_sum = lax.psum_scatter(
        jnp.dot(row_piece, out_used, preferred_element_type=jnp.float32).astype(jnp.bfloat16),
        "tp",
        scatter_dimension=0,
        tiled=True,
    ).astype(jnp.float32)
    layer_out = (tokens.astype(jnp.float32) + head_sum).astype(jnp.bfloat16)
    grad_rows = lax.all_gather(cotangent, "tp", axis=0, tiled=True)
    grad_attended = jnp.einsum("tm,fm->tf", grad_rows, out_used, preferred_element_type=jnp.float32)
    grad_attended = grad_attended.reshape(block_rows, local_heads, head_width)
    inner_mean = jnp.mean(grad_attended * normed, axis=-1, keepdims=True)
    grad_mixed = inv_rms * (grad_attended - normed * inner_mean)
    grad_low = grad_mixed.astype(jnp.bfloat16)
    local_adjoint = jnp.einsum("thd,the->hde", query_wide, grad_mixed, precision=highest)
    after_state = entering(local_adjoint, "ctx", add_states, zeros_state)
    adjoint_scores = jnp.einsum(
        "the,she->hts", grad_low, values, preferred_element_type=jnp.float32
    )
    adjoint_scores = jnp.where(causal_keep, adjoint_scores, 0.0).astype(jnp.bfloat16)
    grad_query = jnp.einsum(
        "hts,shd->thd", adjoint_scores, key_spiked, preferred_element_type=jnp.float32
    )
    grad_query = grad_query + jnp.einsum("the,hde->thd", grad_mixed, prior_state, precision=highest)
    grad_key = jnp.einsum(
        "hts,thd->shd", adjoint_scores, query_spiked, preferred_element_type=jnp.float32
    )
    grad_key = grad_key + jnp.einsum(
        "she,hde->shd", values.astype(jnp.float32), after_state, precision=highest
    )
    grad_value = jnp.einsum("hts,the->she", scores, grad_low, preferred_element_type=jnp.float32)
    grad_value = grad_value + jnp.einsum("shd,hde->she", key_wide, after_state, precision=highest)
    grad_proj = jnp.stack(
        [
            (grad_query * query_spikes.astype(jnp.float32)).astype(jnp.bfloat16),
            (grad_key * key_spikes.astype(jnp.float32)).astype(jnp.bfloat16),
            grad_value.astype(jnp.bfloat16),
        ],
        axis=1,
    ).reshape(block_rows, 3 * features)
    row_piece = grad_proj
    token_sum = lax.psum_scatter(
        jnp.einsum("tc,mc->tm", row_piece, qkv_used, preferred_element_type=jnp.float32).astype(
            jnp.bfloat16
        ),
        "tp",
        scatter_dimension=0,
        tiled=True,
    ).astype(jnp.float32)
    token_grad = (cotangent.astype(jnp.float32) + token_sum).astype(jnp.bfloat16)
    out_keep_cols = expand_blocks(jnp.transpose(out_blocks))
    slice_rows = model_width // lax.axis_size("ctx")
    norm_factor = 1.0 / math.sqrt(block_rows * lax.axis_size("ctx"))
    qkv_part = jnp.einsum("tm,tc->mc", gathered, grad_proj, preferred_element_type=jnp.float32)
    qkv_part = qkv_part * qkv_keep
    out_part = jnp.einsum("tm,tf->mf", grad_rows, attended, preferred_element_type=jnp.float32)
    out_part = out_part * out_keep_cols
    weight_sum = lax.psum_scatter(
        jnp.concatenate([qkv_part, out_part], axis=1).astype(jnp.bfloat16),
        "ctx",
        scatter_dimension=0,
        tiled=True,
    ).astype(jnp.float32)
    weight_sum = weight_sum * norm_factor
    qkv_grad = weight_sum[:, : 3 * features].reshape(slice_rows, 3, features)
    out_grad = jnp.transpose(weight_sum[:, 3 * features :])
    return (layer_out, token_grad, qkv_grad, out_grad)


def solution(mesh):
    placed = (
        P(("ctx", "tp"), None),
        P("ctx", "tp"),
        P("ctx", "tp"),
        P(None, None, "tp"),
        P(None, None, "tp"),
        P("tp", None),
        P("tp", None),
        P(("ctx", "tp"), None),
    )
    return jax.shard_map(
        on_device,
        mesh=mesh,
        in_specs=placed,
        out_specs=(
            P(("ctx", "tp"), None),
            P(("ctx", "tp"), None),
            P("ctx", None, "tp"),
            P("tp", "ctx"),
        ),
        check_vma=False,
    )
```

profile of v0, /device:TPU:0, one launch (start us, length us, event | category | flops | bytes accessed | tf_op | source)
XLA Modules:
  0.0 714.5 jit_solution(4649358727200529671)
XLA Ops:
  8.0 32.2 %copy.43 = bf16[4096,3,1024]{0,2,1:T(8,128)(2,1)} copy(bf16[4096,3,1024]{2,0,1:T(8,128)(2,1)} %param.15) | data formatting | bytes 50331648 | tf_op args[3]
  40.2 4.5 broadcast_in_dim.22
  44.7 13.3 %stack_reshape.9 = bf16[4096,1,1024]{0,2,1:T(8,128)(2,1)} reshape(bf16[32,128,8,128]{1,0,3,2:T(8,128)(2,1)} %broadcast_in_dim.22) | data formatting | bytes 16777216 | tf_op jit(solution)/shard_map/stack;reshape | solution.py:48
  58.0 4.5 broadcast_in_dim.25
  62.5 13.3 %stack_reshape.10 = bf16[4096,1,1024]{0,2,1:T(8,128)(2,1)} reshape(bf16[32,128,8,128]{1,0,3,2:T(8,128)(2,1)} %broadcast_in_dim.25) | data formatting | bytes 16777216 | tf_op jit(solution)/shard_map/stack;reshape | solution.py:48
  80.3 13.4 %stack_reshape.11 = bf16[4096,1,1024]{0,2,1:T(8,128)(2,1)} reshape(bf16[32,128,8,128]{1,0,3,2:T(8,128)(2,1)} %broadcast_in_dim.26) | data formatting | bytes 16777216 | tf_op jit(solution)/shard_map/stack;reshape | solution.py:48
  93.7 7.8 %constant_dynamic-update-slice_fusion.2 = bf16[4096,3,1024]{0,2,1:T(8,128)(2,1)} fusion(bf16[4096,1,1024]{0,2,1:T(8,128)(2,1)} %stack_reshape.9), kind=kLoop, calls=%fused_computation.51 | loop fusion | bytes 16777216
  101.5 7.7 %constant_dynamic-update-slice_fusion.1 = bf16[4096,3,1024]{0,2,1:T(8,128)(2,1)} fusion(bf16[4096,3,1024]{0,2,1:T(8,128)(2,1)} %constant_dynamic-update-slice_fusion.2, bf16[4096,1,1024]{0,2,1:T(8,128)(2,1)} %stack_reshape.10), kind=kLoop, calls=%fused_computation.50 | loop fusion | bytes 16777216
  109.2 7.8 %constant_dynamic-update-slice_fusion = bf16[4096,3,1024]{0,2,1:T(8,128)(2,1)} fusion(bf16[4096,3,1024]{0,2,1:T(8,128)(2,1)} %constant_dynamic-update-slice_fusion.1, bf16[4096,1,1024]{0,2,1:T(8,128)(2,1)} %stack_reshape.11), kind=kLoop, calls=%fused_computation.49 | loop fusion | bytes 16777216 | tf_op jit(solution)/shard_map/stack | solution.py:48
  117.0 28.6 %mul.82 = bf16[4096,3,1024]{0,2,1:T(8,128)(2,1)} multiply(bf16[4096,3,1024]{0,2,1:T(8,128)(2,1)} %copy.43, bf16[4096,3,1024]{0,2,1:T(8,128)(2,1)} %constant_dynamic-update-slice_fusion) | non-fusion elementwise | flops 12582912 | bytes 75497472 | tf_op jit(solution)/shard_map/mul | solution.py:65
  145.7 18.2 %convolution_convert_fusion.2 = bf16[3072,512]{1,0:T(8,128)(2,1)S(1)} fusion(bf16[4096,3072]{0,1:T(8,128)(2,1)} %bitcast.148, bf16[512,4096]{1,0:T(8,128)(2,1)} %all-gather.7.cloned.1.call-done), kind=kOutput, calls=%fused_computation.13 | convolution fusion | flops 12886474752 | bytes 32505856 | tf_op jit(solution)/shard_map/dot_general | solution.py:68
  172.7 22.8 %all-gather.11.cloned.1.call-done = bf16[64,128,128]{2,1,0:T(8,128)(2,1)} async-done(((bf16[8,128,128]{2,1,0:T(8,128)(2,1)}), bf16[64,128,128]{2,1,0:T(8,128)(2,1)}) %all-gather.11.cloned.1.call-update) | async-done | bytes 2097168 | tf_op jit(solution)/shard_map/all_gather | solution.py:13
  198.6 79.2 %all-gather.9.cloned.1.call-done = bf16[512,4096]{1,0:T(8,128)(2,1)} async-done(((bf16[128,4096]{1,0:T(8,128)(2,1)}), bf16[512,4096]{1,0:T(8,128)(2,1)}) %all-gather.9.cloned.1.call-update) | async-done | bytes 4194320 | tf_op jit(solution)/shard_map/all_gather | solution.py:99
  279.0 12.4 %multiply_reduce_fusion = (f32[512,8]{0,1:T(8,128)S(1)}, f32[1024,512]{1,0:T(8,128)S(1)}) fusion(f32[8,128,512]{2,1,0:T(8,128)S(1)} %get-tuple-element.125, f32[512,8]{0,1:T(8,128)S(1)} %add_rsqrt_fusion, bf16[512,4096]{1,0:T(8,128)(2,1)} %all-gather.9.cloned.1.call-done, bf16[1024,4096]{1,0:T(8,128)(2,1)} %param.17, bf16[128,8,32,128]{3,2,1,0:T(8,128)(2,1)S(1)} %bitcast.145), kind=kOutput, calls=%fused_computation.27 | convolution fusion | flops 4300730368 | bytes 25198592 | tf_op jit(solution)/shard_map/tm,fm->tf/dot_general | solution.py:100
  298.0 13.5 %convolution_convert_fusion.1 = bf16[512,4096]{1,0:T(8,128)(2,1)} fusion(bf16[512,1024]{0,1:T(8,128)(2,1)} %bitcast.160, bf16[1024,4096]{1,0:T(8,128)(2,1)} %param.17, bf16[128,8,32,128]{3,2,1,0:T(8,128)(2,1)} %bitcast.146), kind=kOutput, calls=%fused_computation.12 | convolution fusion | flops 4301258752 | bytes 22020096 | tf_op jit(solution)/shard_map/dot_general | solution.py:93
  324.3 8.2 %while.23 = (s32[]{:T(128)}, f32[8,128,128]{2,1,0:T(8,128)S(1)}, s32[]{:T(128)}, bf16[8,8,128,128]{3,2,1,0:T(8,128)(2,1)}, s32[]{:T(128)}, /*index=5*/s32[]{:T(128)}, s32[]{:T(128)}, s32[]{:T(128)}) while((s32[]{:T(128)}, f32[8,128,128]{2,1,0:T(8,128)S(1)}, s32[]{:T(128)}, bf16[8,8,128,128]{3,2,1,0:T(8,128)(2,1)}, s32[]{:T(128)}, ...), condition=%wide.region_6.7_spmd, body=%wide.region_5.6_spmd.sunk | while | flops 262150 | bytes 1310863 | solution.py:35
  340.4 19.9 %convolution_convert_fusion = bf16[512,4096]{1,0:T(8,128)(2,1)} fusion(bf16[512,3072]{0,1:T(8,128)(2,1)S(1)} %bitcast.162, bf16[4096,3072]{0,1:T(8,128)(2,1)} %bitcast.149), kind=kOutput, calls=%fused_computation.11 | convolution fusion | flops 12886999040 | bytes 32505856 | tf_op jit(solution)/shard_map/tc,mc->tm/dot_general | solution.py:133
  360.3 8.0 %broadcast_in_dim.58 = f32[32,128,8,128]{1,0,3,2:T(8,128)} broadcast(f32[32,8]{0,1:T(8,128)S(1)} %get-tuple-element.113), dimensions={0,2} | broadcast | bytes 16778240 | tf_op jit(solution)/shard_map/broadcast_in_dim | solution.py:40
  368.3 15.5 %fusion.1 = bf16[4096,1024]{0,1:T(8,128)(2,1)} fusion(f32[128,8,32,128]{3,2,1,0:T(8,128)} %bitcast.143, bf16[512,1024]{0,1:T(8,128)(2,1)S(1)} %bitcast.161, bf16[512,4096]{1,0:T(8,128)(2,1)S(1)} %copy-done.6), kind=kOutput, calls=%fused_computation.6 | convolution fusion | flops 4303355904 | bytes 30408704 | tf_op jit(solution)/shard_map/tm,tf->mf/dot_general | solution.py:146
  383.8 27.2 %fusion = bf16[4096,3072]{0,1:T(8,128)(2,1)} fusion(bf16[4096,3072]{0,1:T(8,128)(2,1)} %bitcast.144, bf16[512,3072]{0,1:T(8,128)(2,1)} %bitcast.163, bf16[512,4096]{1,0:T(8,128)(2,1)} %all-gather.7.cloned.1.call-done), kind=kOutput, calls=%fused_computation.3 | convolution fusion | flops 12922650624 | bytes 57671680 | tf_op jit(solution)/shard_map/tm,tc->mc/dot_general | solution.py:144
  411.0 24.0 %pad_maximum_fusion = bf16[4096,4096]{0,1:T(8,128)(2,1)} fusion(bf16[4096,1024]{0,1:T(8,128)(2,1)} %fusion.1, bf16[4096,3072]{0,1:T(8,128)(2,1)} %fusion), kind=kLoop, calls=%fused_computation.4 | loop fusion | flops 67108864 | bytes 67108864 | tf_op jit(solution)/shard_map/concatenate | solution.py:149
  438.7 44.7 %reduce-scatter.6.cloned.1.call-done = bf16[128,4096]{1,0:T(8,128)(2,1)} async-done(((bf16[512,4096]{1,0:T(8,128)(2,1)}), bf16[128,4096]{1,0:T(8,128)(2,1)}) %reduce-scatter.6.cloned.1.call-update) | async-done | bytes 1048592 | tf_op jit(solution)/shard_map/reduce_scatter | solution.py:132
  485.8 206.9 %reduce-scatter.8.cloned.1.call-done = bf16[512,4096]{0,1:T(8,128)(2,1)} async-done(((bf16[4096,4096]{0,1:T(8,128)(2,1)}), bf16[512,4096]{0,1:T(8,128)(2,1)}) %reduce-scatter.8.cloned.1.call-update) | async-done | bytes 4194320 | tf_op jit(solution)/shard_map/reduce_scatter | solution.py:148
  700.9 6.6 copy.56
  (89 shorter events, 67.4 us)
Async XLA Ops:
  7.2 138.5 %all-gather.7.cloned.1.call-start = ((), (), s32[]{:S(2)}) async-start(), calls=%async_computation.3 | async-start | bytes 5242880 | tf_op jit(solution)/shard_map/all_gather | solution.py:67
  7.9 32.3 %copy-start.15 = (s32[3,32,8]{1,2,0:T(8,128)S(1)}, s32[3,32,8]{1,2,0:T(8,128)}, u32[]{:S(2)}) copy-start(s32[3,32,8]{1,2,0:T(8,128)} %param.16) | copy-start | bytes 9220
  7.9 187.5 %all-gather.11.cloned.1.call-start = ((), (), s32[]{:S(2)}) async-start(), calls=%async_computation.8 | async-start | bytes 2359296 | tf_op jit(solution)/shard_map/all_gather | solution.py:13
  117.0 28.6 %copy-start.13 = (s32[512,8]{0,1:T(8,128)S(1)}, s32[512,8]{0,1:T(8,128)}, u32[]{:S(2)}) copy-start(s32[512,8]{0,1:T(8,128)} %param.13) | copy-start | bytes 49156
  117.0 28.6 %copy-start.14 = (s32[512,8]{0,1:T(8,128)S(1)}, s32[512,8]{0,1:T(8,128)}, u32[]{:S(2)}) copy-start(s32[512,8]{0,1:T(8,128)} %param.14) | copy-start | bytes 49156
  163.8 4.0 copy-start.1
  163.8 2.6 copy-start.16
  165.4 112.4 %all-gather.9.cloned.1.call-start = ((), (), s32[]{:S(2)}) async-start(), calls=%async_computation.5 | async-start | bytes 5242880 | tf_op jit(solution)/shard_map/all_gather | solution.py:99
  166.1 158.2 %all-gather.13.cloned.1.call-start = ((), (), s32[]{:S(2)}) async-start(), calls=%async_computation.9 | async-start | bytes 2359296 | tf_op jit(solution)/shard_map/all_gather | solution.py:26
  167.9 2.0 copy-start.4
  198.6 80.4 %copy-start.3 = (f32[8,128,512]{2,1,0:T(8,128)}, f32[8,128,512]{2,1,0:T(8,128)S(1)}, u32[]{:S(2)}) copy-start(f32[8,128,512]{2,1,0:T(8,128)S(1)} %get-tuple-element.125) | copy-start | bytes 6291460
  279.0 12.4 %copy-start = (bf16[8,128,32,128]{3,2,1,0:T(8,128)(2,1)}, bf16[8,128,32,128]{3,2,1,0:T(8,128)(2,1)S(1)}, u32[]{:S(2)}) copy-start(bf16[8,128,32,128]{3,2,1,0:T(8,128)(2,1)S(1)} %broadcast_in_dim.30) | copy-start | bytes 25165828
  297.7 137.3 %reduce-scatter.4.cloned.1.call-start = ((), (), s32[]{:S(2)}) async-start(), calls=%async_computation.4 | async-start | bytes 5242880 | tf_op jit(solution)/shard_map/reduce_scatter | solution.py:92
  311.5 171.9 %reduce-scatter.6.cloned.1.call-start = ((), (), s32[]{:S(2)}) async-start(), calls=%async_computation.6 | async-start | bytes 5242880 | tf_op jit(solution)/shard_map/reduce_scatter | solution.py:132
  311.5 2.7 copy-start.2
  318.6 3.0 copy-start.5
  324.3 11.8 %copy-start.7 = (f32[8,128,512]{2,1,0:T(8,128)S(1)}, f32[8,128,512]{2,1,0:T(8,128)}, u32[]{:S(2)}) copy-start(f32[8,128,512]{2,1,0:T(8,128)} %fusion.17) | copy-start | bytes 6291460
  332.5 5.8 copy-start.11
  338.7 1.6 copy-start.12
  360.3 332.4 %reduce-scatter.8.cloned.1.call-start = ((), (), s32[]{:S(2)}) async-start(), calls=%async_computation.7 | async-start | bytes 37748736 | tf_op jit(solution)/shard_map/reduce_scatter | solution.py:148
  360.3 8.0 %copy-start.6 = (bf16[512,4096]{1,0:T(8,128)(2,1)S(1)}, bf16[512,4096]{1,0:T(8,128)(2,1)}, u32[]{:S(2)}) copy-start(bf16[512,4096]{1,0:T(8,128)(2,1)} %all-gather.9.cloned.1.call-done) | copy-start | bytes 12582916
  360.3 8.0 %copy-start.8 = (bf16[512,8,128]{0,2,1:T(8,128)(2,1)S(1)}, bf16[512,8,128]{0,2,1:T(8,128)(2,1)}, u32[]{:S(2)}) copy-start(bf16[512,8,128]{0,2,1:T(8,128)(2,1)} %get-tuple-element.120) | copy-start | bytes 3145732
  435.0 1.2 copy-start.9
  435.0 48.4 %copy-start.10 = (bf16[128,4096]{1,0:T(8,128)(2,1)S(1)}, bf16[128,4096]{1,0:T(8,128)(2,1)}, u32[]{:S(2)}) copy-start(bf16[128,4096]{1,0:T(8,128)(2,1)} %param.19) | copy-start | bytes 3145732
Sparse Core Ops, SparseCore 0:
  9.6 83.4 all-gather.6
  165.5 29.8 all-gather.10
  197.0 80.7 all-gather.8
  297.8 26.4 all-gather.12
  327.0 76.7 reduce-scatter.3
  406.1 77.2 reduce-scatter.5
  486.9 205.7 reduce-scatter.7
where the time goes:
time: 725 us; the launch traced here: 715 us
  waiting for transfers between devices  356 us (49%)
  matrix products  136 us (19%)
  local copies, waits for them, and re-layouts  135 us (19%)
  other arithmetic  72 us (10%)
  between operations  14.7 us (2%)
    reduce_scatter x1, waiting for transfers between devices, on_device(): lax.psum_scatter(jnp.concatenate([qkv_part, out_part], axis=1).astype(jnp...  207 us
    all_gather x1, waiting for transfers between devices, on_device(): grad_rows = lax.all_gather(cotangent, 'tp', axis=0, tiled=True)  79.2 us
    unnamed x38, local copies, waits for them, and re-layouts  60 us
    another operation x4, local copies, waits for them, and re-layouts, qkv_keep_table(): return jnp.stack(tables, axis=1)  47.8 us
    reduce_scatter x1, waiting for transfers between devices, on_device(): lax.psum_scatter(jnp.einsum('tc,mc->tm', row_piece, qkv_used, preferred_e...  44.7 us
    mul x1, other arithmetic, on_device(): qkv_used = qkv_weight.reshape(model_width, 3 * features) * qkv_keep  28.6 us
    dot_general x1, matrix products, on_device(): jnp.einsum('tm,tc->mc', gathered, grad_proj, preferred_element_type=jnp.f...  27.2 us
    concatenate x1, other arithmetic, on_device(): jnp.concatenate([qkv_part, out_part], axis=1).astype(jnp.bfloat16)  24 us
  transfers between devices with their start and end apart: 7, of which 5 were waited for; matrix products, arithmetic and copies ran while one was open for 40% of the time, Pallas kernels for 0%

commit v1 on v0

--- a/solution.py
+++ b/solution.py
@@ -96,7 +96,20 @@
         tiled=True,
     ).astype(jnp.float32)
     layer_out = (tokens.astype(jnp.float32) + head_sum).astype(jnp.bfloat16)
-    grad_rows = lax.all_gather(cotangent, "tp", axis=0, tiled=True)
+    parts_n = lax.axis_size("tp")
+    in_order = []
+    for dd in range(parts_n):
+        in_order.append((dd, (dd + 1) % parts_n))
+    vals = []
+    for dd in range(parts_n):
+        vals.append((dd, (dd - 1) % parts_n))
+    near, mid_arr = ([cotangent], [cotangent])
+    for _ in range(parts_n // 2):
+        near.append(lax.ppermute(near[-1], "tp", in_order))
+    for _ in range((parts_n - 1) // 2):
+        mid_arr.append(lax.ppermute(mid_arr[-1], "tp", vals))
+    plain = jnp.concatenate([*near[::-1], *mid_arr[1:]], axis=0)
+    grad_rows = jnp.roll(plain, (lax.axis_index("tp") - parts_n // 2) * cotangent.shape[0], axis=0)
     grad_attended = jnp.einsum("tm,fm->tf", grad_rows, out_used, preferred_element_type=jnp.float32)
     grad_attended = grad_attended.reshape(block_rows, local_heads, head_width)
     inner_mean = jnp.mean(grad_attended * normed, axis=-1, keepdims=True)

time: 725 us -> 665 us (0.917)
  waiting for transfers between devices: 356 us -> 270 us
  local copies, waits for them, and re-layouts: 135 us -> 149 us
  matrix products: 136 us -> 144 us
    all_gather x1 -> x0, waiting for transfers between devices: 79.2 us -> none  [on_device(): grad_rows = lax.all_gather(cotangent, 'tp', axis=0, tiled=True)]
    all_gather x1, waiting for transfers between devices: 22.8 us -> 10.4 us  [carried_in(): gathered = lax.all_gather(value.astype(jnp.bfloat16), axis)]
    unnamed x38 -> x49, local copies, waits for them, and re-layouts: 60 us -> 71.3 us
    all_gather x1, waiting for transfers between devices: 0.59 us -> 9.59 us  [entering(): lax.all_gather(value.astype(jnp.bfloat16 if value.dtype == jnp.float32 el...]
  transfers between devices with their start and end apart: 7 -> 9, of which waited for: 5 -> 4; matrix products, arithmetic and copies ran while one was open for 40% -> 48% of each run, Pallas kernels for 0% -> 0%
where the time goes in v1:
time: 665 us; the launch traced here: 657 us
  waiting for transfers between devices  270 us (41%)
  local copies, waits for them, and re-layouts  149 us (22%)
  matrix products  144 us (22%)
  other arithmetic  72.3 us (11%)
  between operations  14.7 us (2%)
    reduce_scatter x1, waiting for transfers between devices, on_device(): lax.psum_scatter(jnp.concatenate([qkv_part, out_part], axis=1).astype(jnp...  207 us
    unnamed x49, local copies, waits for them, and re-layouts  71.3 us
    another operation x4, local copies, waits for them, and re-layouts, qkv_keep_table(): return jnp.stack(tables, axis=1)  48 us
    reduce_scatter x1, waiting for transfers between devices, on_device(): lax.psum_scatter(jnp.einsum('tc,mc->tm', row_piece, qkv_used, preferred_e...  42.8 us
    mul x1, other arithmetic, on_device(): qkv_used = qkv_weight.reshape(model_width, 3 * features) * qkv_keep  28.6 us
    dot_general x1, matrix products, on_device(): jnp.einsum('tm,tc->mc', gathered, grad_proj, preferred_element_type=jnp.f...  25.8 us
    concatenate x1, other arithmetic, on_device(): jnp.concatenate([qkv_part, out_part], axis=1).astype(jnp.bfloat16)  23.5 us
    broadcast_in_dim x5, local copies, waits for them, and re-layouts, expand_blocks(): jnp.broadcast_to(blocks.astype(jnp.bfloat16)[:, None, :, None], (row_bloc...  22.3 us
  transfers between devices with their start and end apart: 9, of which 4 were waited for; matrix products, arithmetic and copies ran while one was open for 48% of the time, Pallas kernels for 0%

profile of v1, /device:TPU:0, one launch (start us, length us, event | category | flops | bytes accessed | tf_op | source)
XLA Modules:
  0.0 657.1 jit_solution(11349173817752734382)
XLA Ops:
  13.1 33.6 %copy.45 = bf16[4096,3,1024]{0,2,1:T(8,128)(2,1)} copy(bf16[4096,3,1024]{2,0,1:T(8,128)(2,1)} %param.15) | data formatting | bytes 50331648 | tf_op args[3]
  46.7 4.4 broadcast_in_dim.22
  51.1 13.3 %stack_reshape.9 = bf16[4096,1,1024]{0,2,1:T(8,128)(2,1)} reshape(bf16[32,128,8,128]{1,0,3,2:T(8,128)(2,1)} %broadcast_in_dim.22) | data formatting | bytes 16777216 | tf_op jit(solution)/shard_map/stack;reshape | solution.py:48
  68.8 13.3 %stack_reshape.10 = bf16[4096,1,1024]{0,2,1:T(8,128)(2,1)} reshape(bf16[32,128,8,128]{1,0,3,2:T(8,128)(2,1)} %broadcast_in_dim.25) | data formatting | bytes 16777216 | tf_op jit(solution)/shard_map/stack;reshape | solution.py:48
  82.2 4.4 broadcast_in_dim.26
  86.6 13.3 %stack_reshape.11 = bf16[4096,1,1024]{0,2,1:T(8,128)(2,1)} reshape(bf16[32,128,8,128]{1,0,3,2:T(8,128)(2,1)} %broadcast_in_dim.26) | data formatting | bytes 16777216 | tf_op jit(solution)/shard_map/stack;reshape | solution.py:48
  99.9 7.7 %constant_dynamic-update-slice_fusion.2 = bf16[4096,3,1024]{0,2,1:T(8,128)(2,1)} fusion(bf16[4096,1,1024]{0,2,1:T(8,128)(2,1)} %stack_reshape.9), kind=kLoop, calls=%fused_computation.52 | loop fusion | bytes 16777216
  107.6 7.7 %constant_dynamic-update-slice_fusion.1 = bf16[4096,3,1024]{0,2,1:T(8,128)(2,1)} fusion(bf16[4096,3,1024]{0,2,1:T(8,128)(2,1)} %constant_dynamic-update-slice_fusion.2, bf16[4096,1,1024]{0,2,1:T(8,128)(2,1)} %stack_reshape.10), kind=kLoop, calls=%fused_computation.51 | loop fusion | bytes 16777216
  115.6 8.0 %constant_dynamic-update-slice_fusion = bf16[4096,3,1024]{0,2,1:T(8,128)(2,1)} fusion(bf16[4096,3,1024]{0,2,1:T(8,128)(2,1)} %constant_dynamic-update-slice_fusion.1, bf16[4096,1,1024]{0,2,1:T(8,128)(2,1)} %stack_reshape.11), kind=kLoop, calls=%fused_computation.50 | loop fusion | bytes 16777216 | tf_op jit(solution)/shard_map/stack | solution.py:48
  123.6 28.6 %mul.85 = bf16[4096,3,1024]{0,2,1:T(8,128)(2,1)} multiply(bf16[4096,3,1024]{0,2,1:T(8,128)(2,1)} %copy.45, bf16[4096,3,1024]{0,2,1:T(8,128)(2,1)} %constant_dynamic-update-slice_fusion) | non-fusion elementwise | flops 12582912 | bytes 75497472 | tf_op jit(solution)/shard_map/mul | solution.py:65
  153.7 18.2 %convolution_convert_fusion.2 = bf16[3072,512]{1,0:T(8,128)(2,1)S(1)} fusion(bf16[4096,3072]{0,1:T(8,128)(2,1)} %bitcast.142, bf16[512,4096]{1,0:T(8,128)(2,1)} %all-gather.6.cloned.1.call-done), kind=kOutput, calls=%fused_computation.13 | convolution fusion | flops 12886474752 | bytes 32505856 | tf_op jit(solution)/shard_map/dot_general | solution.py:68
  192.4 10.4 %all-gather.8.cloned.1.call-done = bf16[64,128,128]{2,1,0:T(8,128)(2,1)} async-done(((bf16[8,128,128]{2,1,0:T(8,128)(2,1)}), bf16[64,128,128]{2,1,0:T(8,128)(2,1)}) %all-gather.8.cloned.1.call-update) | async-done | bytes 2097168 | tf_op jit(solution)/shard_map/all_gather | solution.py:13
  208.6 15.7 %multiply_reduce_fusion = (f32[512,8]{0,1:T(8,128)S(1)}, f32[512,1024]{0,1:T(8,128)}) fusion(f32[8,128,512]{2,1,0:T(8,128)} %get-tuple-element.125, f32[512,8]{0,1:T(8,128)S(1)} %add_rsqrt_fusion, bf16[1024,4096]{1,0:T(8,128)(2,1)} %param.17, bf16[128,8,32,128]{3,2,1,0:T(8,128)(2,1)S(1)} %bitcast.139, ...), kind=kOutput, calls=%fused_computation.29 | convolution fusion | flops 4300730368 | bytes 25198596 | tf_op jit(solution)/shard_map/tm,fm->tf/dot_general | solution.py:113
  231.8 13.3 %convolution_convert_fusion.1 = bf16[512,4096]{1,0:T(8,128)(2,1)} fusion(bf16[512,1024]{0,1:T(8,128)(2,1)} %bitcast.154, bf16[1024,4096]{1,0:T(8,128)(2,1)} %param.17, bf16[128,8,32,128]{3,2,1,0:T(8,128)(2,1)} %bitcast.140), kind=kOutput, calls=%fused_computation.12 | convolution fusion | flops 4301258752 | bytes 22020096 | tf_op jit(solution)/shard_map/dot_general | solution.py:93
  257.3 9.6 %all-gather.10.cloned.1.call-done = bf16[64,128,128]{2,1,0:T(8,128)(2,1)} async-done(((bf16[8,128,128]{2,1,0:T(8,128)(2,1)}), bf16[64,128,128]{2,1,0:T(8,128)(2,1)}) %all-gather.10.cloned.1.call-update) | async-done | bytes 2097168 | tf_op jit(solution)/shard_map/all_gather | solution.py:26
  267.0 8.0 %while.23 = (s32[]{:T(128)}, f32[8,128,128]{2,1,0:T(8,128)S(1)}, s32[]{:T(128)}, bf16[8,8,128,128]{3,2,1,0:T(8,128)(2,1)}, s32[]{:T(128)}, /*index=5*/s32[]{:T(128)}, s32[]{:T(128)}, s32[]{:T(128)}) while((s32[]{:T(128)}, f32[8,128,128]{2,1,0:T(8,128)S(1)}, s32[]{:T(128)}, bf16[8,8,128,128]{3,2,1,0:T(8,128)(2,1)}, s32[]{:T(128)}, ...), condition=%wide.region_6.7_spmd, body=%wide.region_5.6_spmd.sunk | while | flops 262150 | bytes 1310863 | solution.py:35
  281.2 19.5 %convolution_convert_fusion = bf16[512,4096]{1,0:T(8,128)(2,1)} fusion(bf16[512,3072]{0,1:T(8,128)(2,1)S(1)} %bitcast.156, bf16[4096,3072]{0,1:T(8,128)(2,1)} %bitcast.143), kind=kOutput, calls=%fused_computation.11 | convolution fusion | flops 12886999040 | bytes 32505856 | tf_op jit(solution)/shard_map/tc,mc->tm/dot_general | solution.py:146
  301.1 8.0 %broadcast_in_dim.58 = f32[32,128,8,128]{1,0,3,2:T(8,128)} broadcast(f32[32,8]{0,1:T(8,128)S(1)} %get-tuple-element.113), dimensions={0,2} | broadcast | bytes 16778240 | tf_op jit(solution)/shard_map/broadcast_in_dim | solution.py:40
  309.0 21.2 %fusion.1 = bf16[4096,1024]{0,1:T(8,128)(2,1)} fusion(f32[128,8,32,128]{3,2,1,0:T(8,128)} %bitcast.137, bf16[512,1024]{0,1:T(8,128)(2,1)S(1)} %bitcast.155, bf16[1024,4096]{1,0:T(8,128)(2,1)} %constant_dynamic-update-slice_fusion.3, s32[]{:T(128)S(6)} %select_n.33), kind=kOutput, calls=%fused_computation.6 | convolution fusion | flops 4303355904 | bytes 30408708 | tf_op jit(solution)/shard_map/tm,tf->mf/dot_general | solution.py:159
  330.2 25.8 %fusion = bf16[4096,3072]{0,1:T(8,128)(2,1)} fusion(bf16[4096,3072]{0,1:T(8,128)(2,1)} %bitcast.138, bf16[512,3072]{0,1:T(8,128)(2,1)S(1)} %bitcast.157, bf16[512,4096]{1,0:T(8,128)(2,1)} %all-gather.6.cloned.1.call-done), kind=kOutput, calls=%fused_computation.3 | convolution fusion | flops 12922650624 | bytes 57671680 | tf_op jit(solution)/shard_map/tm,tc->mc/dot_general | solution.py:157
  356.0 23.5 %pad_maximum_fusion = bf16[4096,4096]{0,1:T(8,128)(2,1)} fusion(bf16[4096,1024]{0,1:T(8,128)(2,1)} %fusion.1, bf16[4096,3072]{0,1:T(8,128)(2,1)} %fusion), kind=kLoop, calls=%fused_computation.4 | loop fusion | flops 67108864 | bytes 67108864 | tf_op jit(solution)/shard_map/concatenate | solution.py:162
  383.2 42.8 %reduce-scatter.6.cloned.1.call-done = bf16[128,4096]{1,0:T(8,128)(2,1)} async-done(((bf16[512,4096]{1,0:T(8,128)(2,1)}), bf16[128,4096]{1,0:T(8,128)(2,1)}) %reduce-scatter.6.cloned.1.call-update) | async-done | bytes 1048592 | tf_op jit(solution)/shard_map/reduce_scatter | solution.py:145
  428.4 206.8 %reduce-scatter.8.cloned.1.call-done = bf16[512,4096]{0,1:T(8,128)(2,1)} async-done(((bf16[4096,4096]{0,1:T(8,128)(2,1)}), bf16[512,4096]{0,1:T(8,128)(2,1)}) %reduce-scatter.8.cloned.1.call-update) | async-done | bytes 4194320 | tf_op jit(solution)/shard_map/reduce_scatter | solution.py:161
  643.4 6.6 copy.59
  (104 shorter events, 86.3 us)
Async XLA Ops:
  7.2 146.4 %all-gather.6.cloned.1.call-start = ((), (), s32[]{:S(2)}) async-start(), calls=%async_computation.3 | async-start | bytes 5242880 | tf_op jit(solution)/shard_map/all_gather | solution.py:67
  7.9 194.9 %all-gather.8.cloned.1.call-start = ((), (), s32[]{:S(2)}) async-start(), calls=%async_computation.7 | async-start | bytes 2359296 | tf_op jit(solution)/shard_map/all_gather | solution.py:13
  7.9 107.4 %collective-permute-start = (bf16[128,4096]{1,0:T(8,128)(2,1)}, bf16[128,4096]{1,0:T(8,128)(2,1)S(1)}, u32[]{:S(2)}, u32[]{:S(2)}) collective-permute-start(bf16[128,4096]{1,0:T(8,128)(2,1)} %param.19), channel_id=1, source_target_pairs={{0,1},{1,2},{2,3},{3,0},{4,5},{5,6},{6,7},{7,4},{8,9},{9,10},{10,1... | collective-permute-start | bytes 3145736 | tf_op jit(solution)/shard_map/ppermute | solution.py:108
  11.0 167.3 %collective-permute-start.2 = (bf16[128,4096]{1,0:T(8,128)(2,1)}, bf16[128,4096]{1,0:T(8,128)(2,1)}, u32[]{:S(2)}, u32[]{:S(2)}) collective-permute-start(bf16[128,4096]{1,0:T(8,128)(2,1)} %param.19), channel_id=1, source_target_pairs={{0,3},{1,0},{2,1},{3,2},{4,7},{5,4},{6,5},{7,6},{8,11},{9,8},{10,9... | collective-permute-start | bytes 3145736 | tf_op jit(solution)/shard_map/ppermute | solution.py:110
  13.1 33.6 %copy-start.17 = (s32[3,32,8]{1,2,0:T(8,128)S(1)}, s32[3,32,8]{1,2,0:T(8,128)}, u32[]{:S(2)}) copy-start(s32[3,32,8]{1,2,0:T(8,128)} %param.16) | copy-start | bytes 9220
  115.4 8.2 %copy-start.10 = (bf16[128,4096]{1,0:T(8,128)(2,1)}, bf16[128,4096]{1,0:T(8,128)(2,1)S(1)}, u32[]{:S(2)}) copy-start(bf16[128,4096]{1,0:T(8,128)(2,1)S(1)} %collective-permute-done) | copy-start | bytes 3145732
  115.4 37.0 %collective-permute-start.1 = (bf16[128,4096]{1,0:T(8,128)(2,1)S(1)}, bf16[128,4096]{1,0:T(8,128)(2,1)S(1)}, u32[]{:S(2)}, u32[]{:S(2)}) collective-permute-start(bf16[128,4096]{1,0:T(8,128)(2,1)S(1)} %collective-permute-done), channel_id=1, source_target_pairs={{0,1},{1,2},{2,3},{3,0},{4,5},{5,6},{6,7},{7,4},{8,9},{9,10},{10,1... | collective-permute-start | bytes 3145736 | tf_op jit(solution)/shard_map/ppermute | solution.py:108
  123.6 28.7 %copy-start.18 = (s32[8,32]{1,0:T(8,128)S(1)}, s32[8,32]{1,0:T(8,128)}, u32[]{:S(2)}) copy-start(s32[8,32]{1,0:T(8,128)} %param.18) | copy-start | bytes 3076
  123.6 28.7 %copy-start.15 = (s32[512,8]{0,1:T(8,128)S(1)}, s32[512,8]{0,1:T(8,128)}, u32[]{:S(2)}) copy-start(s32[512,8]{0,1:T(8,128)} %param.13) | copy-start | bytes 49156
  123.6 28.8 %copy-start.16 = (s32[512,8]{0,1:T(8,128)S(1)}, s32[512,8]{0,1:T(8,128)}, u32[]{:S(2)}) copy-start(s32[512,8]{0,1:T(8,128)} %param.14) | copy-start | bytes 49156
  171.9 15.7 %copy-start.1 = (bf16[3072,512]{1,0:T(8,128)(2,1)}, bf16[3072,512]{1,0:T(8,128)(2,1)S(1)}, u32[]{:S(2)}) copy-start(bf16[3072,512]{1,0:T(8,128)(2,1)S(1)} %convolution_convert_fusion.2) | copy-start | bytes 9437188
  173.4 93.5 %all-gather.10.cloned.1.call-start = ((), (), s32[]{:S(2)}) async-start(), calls=%async_computation.8 | async-start | bytes 2359296 | tf_op jit(solution)/shard_map/all_gather | solution.py:26
  173.4 7.2 %copy-start.13 = (bf16[128,4096]{1,0:T(8,128)(2,1)S(1)}, bf16[128,4096]{1,0:T(8,128)(2,1)}, u32[]{:S(2)}) copy-start(bf16[128,4096]{1,0:T(8,128)(2,1)} %copy-done.12) | copy-start | bytes 3145732
  173.5 8.3 %copy-start.11 = (bf16[128,4096]{1,0:T(8,128)(2,1)S(1)}, bf16[128,4096]{1,0:T(8,128)(2,1)}, u32[]{:S(2)}) copy-start(bf16[128,4096]{1,0:T(8,128)(2,1)} %copy-done.10) | copy-start | bytes 3145732
  175.9 6.8 %copy-start.5 = (bf16[128,4096]{1,0:T(8,128)(2,1)S(1)}, bf16[128,4096]{1,0:T(8,128)(2,1)}, u32[]{:S(2)}) copy-start(bf16[128,4096]{1,0:T(8,128)(2,1)} %param.19) | copy-start | bytes 3145732
  208.6 15.7 %copy-start = (bf16[8,128,32,128]{3,2,1,0:T(8,128)(2,1)}, bf16[8,128,32,128]{3,2,1,0:T(8,128)(2,1)S(1)}, u32[]{:S(2)}) copy-start(bf16[8,128,32,128]{3,2,1,0:T(8,128)(2,1)S(1)} %broadcast_in_dim.30) | copy-start | bytes 25165828
  231.4 148.3 %reduce-scatter.4.cloned.1.call-start = ((), (), s32[]{:S(2)}) async-start(), calls=%async_computation.4 | async-start | bytes 5242880 | tf_op jit(solution)/shard_map/reduce_scatter | solution.py:92
  245.1 180.8 %reduce-scatter.6.cloned.1.call-start = ((), (), s32[]{:S(2)}) async-start(), calls=%async_computation.5 | async-start | bytes 5242880 | tf_op jit(solution)/shard_map/reduce_scatter | solution.py:145
  252.3 2.9 copy-start.4
  267.0 11.6 %copy-start.7 = (f32[8,128,512]{2,1,0:T(8,128)S(1)}, f32[8,128,512]{2,1,0:T(8,128)}, u32[]{:S(2)}) copy-start(f32[8,128,512]{2,1,0:T(8,128)} %fusion.19) | copy-start | bytes 6291460
  275.0 5.9 copy-start.14
  300.8 334.4 %reduce-scatter.8.cloned.1.call-start = ((), (), s32[]{:S(2)}) async-start(), calls=%async_computation.6 | async-start | bytes 37748736 | tf_op jit(solution)/shard_map/reduce_scatter | solution.py:161
  301.1 8.0 %copy-start.8 = (bf16[512,8,128]{0,2,1:T(8,128)(2,1)S(1)}, bf16[512,8,128]{0,2,1:T(8,128)(2,1)}, u32[]{:S(2)}) copy-start(bf16[512,8,128]{0,2,1:T(8,128)(2,1)} %get-tuple-element.120) | copy-start | bytes 3145732
  379.6 46.4 %copy-start.6 = (bf16[128,4096]{1,0:T(8,128)(2,1)S(1)}, bf16[128,4096]{1,0:T(8,128)(2,1)}, u32[]{:S(2)}) copy-start(bf16[128,4096]{1,0:T(8,128)(2,1)} %param.19) | copy-start | bytes 3145732
  (4 other events, 7.3 us)
Sparse Core Ops, SparseCore 0:
  9.6 123.7 all-gather.5
  173.5 29.2 all-gather.7
  231.5 35.4 all-gather.9
  269.6 76.7 reduce-scatter.3
  348.7 77.2 reduce-scatter.5
  429.4 205.7 reduce-scatter.7
